TPU v7x, 128 devices: a whole 4x4x4 slice. The times are simulated.
128 devices in a mesh: req: 32 (over z, y, x_lo), tp: 4 (over x_hi, core).
Axes of the slice: x: 4 (x_hi: 2, x_lo: 2; x = x_hi * 2 + x_lo), y: 4, z: 4, core: 2. Of those that a mesh axis runs over, the one named last changes fastest.
Arguments:
- tokens: bfloat16 [16384, 4096], P('req', 'tp'), may hold values from -400 to 400
- input_norm_gain: float32 [4096], replicated, may hold values from 0.1 to 1.9
- query_weight: bfloat16 [4096, 2048], P(None, 'tp'), may hold values from -0.078125 to 0.078125
- key_weight: bfloat16 [4096, 2048], P(None, 'tp'), may hold values from -1.953125 to 1.953125
- value_weight: bfloat16 [4096, 2048], P(None, 'tp'), may hold values from -0.09375 to 0.09375
- query_down_maps: bfloat16 [4096, 512], replicated, may hold values from -0.09375 to 0.09375
- value_down_maps: bfloat16 [4096, 512], replicated, may hold values from -0.09375 to 0.09375
- query_up_maps: bfloat16 [512, 2048], P(None, 'tp'), may hold values from -1.5 to 1.5
- value_up_maps: bfloat16 [512, 2048], P(None, 'tp'), may hold values from -1.5 to 1.5
- lengths: int32 [16], replicated, may hold values from 1 to 8448, 16384 in all
- prompt_adapter_index: int32 [16], replicated, may hold values from 0 to 31
Outputs:
- attended: bfloat16 [16384, 2048], P('req', 'tp')
Inputs may be any that keep to these rules, and one draw needn't show every extreme that they name: `lengths`: the longest prompt has exactly 8448 tokens.
All inputs are finite; a program needn't handle non-finite values.
Results may differ from a plain program's by a relative error of at most 0.0083.
Values may be sent and summed in bfloat16 or wider, within the bound.
No kernel may reach another device: no remote copies, remote signals or barrier semaphores. Data moves between devices by JAX's collectives and lax.ppermute only.
A program may use at most 192 MiB of HBM per device.

v0:
```python
import functools
import math

import jax
import jax.numpy as jnp
from jax import lax
from jax.experimental import pallas as pl
from jax.experimental.pallas import tpu as pltpu
from jax.sharding import PartitionSpec as P

HEAD = 128
ADAPTER_RANK = 16
ADAPTER_COUNT = 32


EPS = 1e-05
ADAPTER_SCALE = 0.5
MASKED = -1e30


def prompt_layout(lengths, positions):
    ends = jnp.cumsum(lengths)
    before = (ends[None, :] <= positions[:, None]).astype(jnp.int32)
    starts = jnp.sum(before * lengths[None, :], axis=1)
    prompt = jnp.sum(before, axis=1)
    return (starts, prompt)


def adapter_mask(prompt, prompt_adapter_index, count, rank):
    chosen = (
        prompt[:, None] == jnp.arange(prompt_adapter_index.shape[0], dtype=jnp.int32)[None, :]
    ).astype(jnp.int32)
    adapter = jnp.sum(chosen * prompt_adapter_index[None, :], axis=1)
    column = jnp.arange(count * rank, dtype=jnp.int32) // rank
    return (column[None, :] == adapter[:, None]).astype(jnp.float32)


def rotate(field, offsets, width):
    half = width // 2
    freq = jnp.exp(jnp.arange(half, dtype=jnp.float32) * (-2.0 * math.log(10000.0) / width))
    angle = offsets.astype(jnp.float32)[:, None] * freq[None, :]
    cosine = jnp.cos(angle)[:, None, :]
    sine = jnp.sin(angle)[:, None, :]
    first = field[..., :half]
    second = field[..., half:]
    return jnp.concatenate(
        [first * cosine - second * sine, second * cosine + first * sine], axis=-1
    )


MAXLEN = 8448

QUERY_TILE = 1024
KEY_TILE = 512


def flash_kernel(meta, q_ref, k_ref, v_ref, start_ref, o_ref, peak_ref, total_ref, acc_ref):
    i = pl.program_id(0)
    j = pl.program_id(1)
    lo = meta[2 + 2 * i]
    hi = meta[3 + 2 * i]

    @pl.when(j == 0)
    def _():
        peak_ref[...] = jnp.full(peak_ref.shape, MASKED, jnp.float32)
        total_ref[...] = jnp.zeros(total_ref.shape, jnp.float32)
        acc_ref[...] = jnp.zeros(acc_ref.shape, jnp.float32)

    @pl.when(lo + j <= hi)
    def _():
        block = lo + j
        scores = lax.dot_general(
            q_ref[...], k_ref[...], (((1,), (1,)), ((), ())), preferred_element_type=jnp.float32
        ) * (1.0 / math.sqrt(HEAD))
        q_pos = meta[0] + i * QUERY_TILE + lax.broadcasted_iota(jnp.int32, (QUERY_TILE, 1), 0)
        k_pos = meta[1] + block * KEY_TILE + lax.broadcasted_iota(jnp.int32, (1, KEY_TILE), 1)
        allowed = (k_pos >= start_ref[...]) & (k_pos <= q_pos)
        scores = jnp.where(allowed, scores, MASKED)
        peak = peak_ref[...]
        new_peak = jnp.maximum(peak, jnp.max(scores, axis=1, keepdims=True))
        weights = jnp.where(allowed, jnp.exp(scores - new_peak), 0.0)
        factor = jnp.exp(peak - new_peak)
        total_ref[...] = total_ref[...] * factor + jnp.sum(weights, axis=1, keepdims=True)
        acc_ref[...] = acc_ref[...] * factor + jnp.dot(
            weights.astype(jnp.bfloat16), v_ref[...], preferred_element_type=jnp.float32
        )
        peak_ref[...] = new_peak

    @pl.when(j == pl.num_programs(1) - 1)
    def _():
        o_ref[...] = (acc_ref[...] / total_ref[...]).astype(o_ref.dtype)


def flash_attention(queries, keys, values, query_first, key_base, lengths):
    query_rows = queries.shape[0]
    key_rows = keys.shape[0]
    q_tiles = query_rows // QUERY_TILE
    k_tiles = key_rows // KEY_TILE
    positions = query_first + jnp.arange(query_rows, dtype=jnp.int32)
    starts, _ = prompt_layout(lengths, positions)
    tile_first = starts[::QUERY_TILE]
    tile_last = positions[QUERY_TILE - 1 :: QUERY_TILE]
    lo = jnp.clip((tile_first - key_base) // KEY_TILE, 0, k_tiles - 1)
    hi = jnp.clip((tile_last - key_base) // KEY_TILE, 0, k_tiles - 1)
    meta = jnp.concatenate(
        [jnp.stack([query_first, key_base]).astype(jnp.int32), jnp.stack([lo, hi], 1).reshape(-1)]
    ).astype(jnp.int32)

    def key_map(i, j, meta):
        return (jnp.minimum(meta[2 + 2 * i] + j, meta[3 + 2 * i]), 0)

    grid_spec = pltpu.PrefetchScalarGridSpec(
        num_scalar_prefetch=1,
        grid=(q_tiles, k_tiles),
        in_specs=[
            pl.BlockSpec((QUERY_TILE, HEAD), lambda i, j, meta: (i, 0)),
            pl.BlockSpec((KEY_TILE, HEAD), key_map),
            pl.BlockSpec((KEY_TILE, HEAD), key_map),
            pl.BlockSpec((QUERY_TILE, 1), lambda i, j, meta: (i, 0)),
        ],
        out_specs=pl.BlockSpec((QUERY_TILE, HEAD), lambda i, j, meta: (i, 0)),
        scratch_shapes=[
            pltpu.VMEM((QUERY_TILE, 1), jnp.float32),
            pltpu.VMEM((QUERY_TILE, 1), jnp.float32),
            pltpu.VMEM((QUERY_TILE, HEAD), jnp.float32),
        ],
    )
    return pl.pallas_call(
        flash_kernel,
        grid_spec=grid_spec,
        out_shape=jax.ShapeDtypeStruct((query_rows, HEAD), jnp.bfloat16),
        compiler_params=pltpu.CompilerParams(
            dimension_semantics=("arbitrary", "arbitrary"), vmem_limit_bytes=48 * 1024 * 1024
        ),
    )(meta, queries, keys, values, starts.reshape(query_rows, 1))


def body(
    req_count,
    tokens,
    input_norm_gain,
    query_weight,
    key_weight,
    value_weight,
    query_down_maps,
    value_down_maps,
    query_up_maps,
    value_up_maps,
    lengths,
    prompt_adapter_index,
):
    row_count = tokens.shape[0]
    req_index = lax.axis_index("req")
    positions = req_index * row_count + jnp.arange(row_count, dtype=jnp.int32)
    starts, prompt = prompt_layout(lengths, positions)
    causal_mask = adapter_mask(prompt, prompt_adapter_index, ADAPTER_COUNT, ADAPTER_RANK)
    incoming_weights = (query_weight, key_weight, value_weight, query_down_maps, value_down_maps)
    whole = lax.all_gather(tokens, "tp", axis=1, tiled=True)
    whole_float = whole.astype(jnp.float32)
    normed = (
        whole_float
        * lax.rsqrt(jnp.mean(whole_float * whole_float, axis=1, keepdims=True) + EPS)
        * input_norm_gain[None, :]
    ).astype(jnp.bfloat16)
    projected = tuple(
        (jnp.dot(normed, weight, preferred_element_type=jnp.float32) for weight in incoming_weights)
    )
    query_linear, key_lin, value_linear, query_middle, value_middle = projected
    query_middle = (query_middle * causal_mask).astype(jnp.bfloat16)
    value_middle = (value_middle * causal_mask).astype(jnp.bfloat16)
    query_linear = query_linear + ADAPTER_SCALE * jnp.dot(
        query_middle, query_up_maps, preferred_element_type=jnp.float32
    )
    value_rows = (
        value_linear
        + ADAPTER_SCALE * jnp.dot(value_middle, value_up_maps, preferred_element_type=jnp.float32)
    ).astype(jnp.bfloat16)
    head_count = query_linear.shape[1] // HEAD
    offsets = positions - starts
    queries = rotate(query_linear.reshape(row_count, head_count, HEAD), offsets, HEAD).astype(
        jnp.bfloat16
    )
    keys = rotate(key_lin.reshape(row_count, head_count, HEAD), offsets, HEAD).astype(jnp.bfloat16)
    values = value_rows.reshape(row_count, head_count, HEAD)
    scale = 1.0 / math.sqrt(HEAD)

    group = head_count
    span = group * row_count
    member = req_index % group
    chunk = req_index // group

    def group_pairs(step):
        return [
            (b * group + i, b * group + (i + step) % group)
            for b in range(req_count // group)
            for i in range(group)
        ]

    def regroup(parts, axis):
        order = (member - jnp.arange(group, dtype=jnp.int32)) % group
        return jnp.take(jnp.stack(parts), order, axis=axis)

    qkv = jnp.stack([queries, keys, values])
    parts = [lax.dynamic_index_in_dim(qkv, member, axis=2, keepdims=False)]
    for step in range(1, group):
        sent = lax.dynamic_index_in_dim(qkv, (member + step) % group, axis=2, keepdims=False)
        parts.append(lax.ppermute(sent, "req", group_pairs(step)))
    local = regroup(parts, 0)
    local = jnp.transpose(local, (1, 0, 2, 3)).reshape(3, span, HEAD)
    query_span = local[0]
    key_value = local[1:]

    chunk_count = req_count // group
    reach = MAXLEN - 1
    segments = [key_value]
    for back in range(1, chunk_count):
        if (back - 1) * span >= reach:
            break
        rows = min(span, -(-(reach - (back - 1) * span) // KEY_TILE) * KEY_TILE)
        pairs = [(i, i + back * group) for i in range(req_count - back * group)]
        segments.insert(0, lax.ppermute(key_value[:, span - rows :], "req", pairs))
    window = jnp.concatenate(segments, axis=1)
    key_base = chunk * span + span - window.shape[1]
    attended = flash_attention(query_span, window[0], window[1], chunk * span, key_base, lengths)
    attended = attended.reshape(group, row_count, HEAD)

    parts = [lax.dynamic_index_in_dim(attended, member, axis=0, keepdims=False)]
    for step in range(1, group):
        sent = lax.dynamic_index_in_dim(attended, (member + step) % group, axis=0, keepdims=False)
        parts.append(lax.ppermute(sent, "req", group_pairs(step)))
    out = regroup(parts, 0)
    return jnp.transpose(out, (1, 0, 2)).reshape(row_count, head_count * HEAD)


def solution(mesh):
    in_specs = (
        P("req", "tp"),
        P(),
        P(None, "tp"),
        P(None, "tp"),
        P(None, "tp"),
        P(),
        P(),
        P(None, "tp"),
        P(None, "tp"),
        P(),
        P(),
    )
    out_specs = P("req", "tp")
    fn = functools.partial(body, mesh.shape["req"])
    return jax.shard_map(fn, mesh=mesh, in_specs=in_specs, out_specs=out_specs, check_vma=False)
```

profile of v0, /device:TPU:64, one launch (start us, length us, event | category | flops | bytes accessed | tf_op | source)
XLA Modules:
  0.0 259.6 jit_solution(6326643991133896469)
XLA Ops:
  6.5 0.7 all-gather.2.cloned.1.call-update
  7.3 0.7 copy.24
  8.3 0.7 fusion.19
  9.0 0.7 select_reduce_fusion.1
  9.8 1.2 multiply_cosine_fusion
  11.0 38.2 %all-gather.2.cloned.1.call-done = bf16[512,4096]{1,0:T(8,128)(2,1)} async-done(((bf16[512,1024]{1,0:T(8,128)(2,1)}), bf16[512,4096]{1,0:T(8,128)(2,1)}) %all-gather.2.cloned.1.call-update) | async-done | bytes 4194320 | tf_op jit(solution)/shard_map/all_gather | solution.py:158
  49.2 3.2 %fusion = f32[512]{0:T(512)S(1)} fusion(bf16[512,4096]{1,0:T(8,128)(2,1)} %all-gather.2.cloned.1.call-done), kind=kLoop, calls=%fused_computation.4 | loop fusion | flops 6290944 | bytes 4196352 | tf_op jit(solution)/shard_map/reduce_sum | solution.py:162
  52.6 5.9 %fusion.36 = f32[512,512]{0,1:T(8,128)} fusion(bf16[4096,512]{1,0:T(8,128)(2,1)} %param.13, bf16[512,4096]{1,0:T(8,128)(2,1)S(1)} %copy-done.1, f32[4096]{0:T(1024)S(1)} %copy-done.8, f32[512]{0:T(512)S(1)} %add_rsqrt_fusion), kind=kOutput, calls=%fused_computation.102 | convolution fusion | flops 2155872256 | bytes 9455616 | tf_op jit(solution)/shard_map/dot_general | solution.py:166
  58.5 2.6 %fusion.32 = f32[512,512]{0,1:T(8,128)S(1)} fusion(bf16[4096,512]{1,0:T(8,128)(2,1)S(1)} %copy-done.6, bf16[512,4096]{1,0:T(8,128)(2,1)S(1)} %copy-done.1, f32[4096]{0:T(1024)S(1)} %copy-done.8, f32[512]{0:T(512)S(1)} %add_rsqrt_fusion), kind=kOutput, calls=%fused_computation.101 | convolution fusion | flops 2155872256 | bytes 9455616 | tf_op jit(solution)/shard_map/dot_general | solution.py:166
  61.1 6.5 %fusion.4 = f32[512,512]{0,1:T(8,128)S(1)} fusion(f32[512,512]{0,1:T(8,128)} %fusion.36, bf16[512,512]{1,0:T(8,128)(2,1)S(1)} %copy-done, bf16[4096,512]{1,0:T(8,128)(2,1)} %param.16, s32[512]{0:T(512)S(1)} %add_select_fusion, s32[512]{0:T(512)S(1)} %select_reduce_fusion.1, bf16[512,4096]{1,0:T(8,128)(2,1)} %all-gather.2.cloned.1.call-done, ...), kind=kOutput, calls=%fused_computation.15 | convolution fusion | flops 2425618432 | bytes 11032576 | tf_op jit(solution)/shard_map/dot_general | solution.py:171
  67.6 2.0 fusion.14
  69.6 7.1 %fusion.30 = f32[512,512]{0,1:T(8,128)} fusion(bf16[4096,512]{1,0:T(8,128)(2,1)} %param.15, bf16[512,4096]{1,0:T(8,128)(2,1)} %all-gather.2.cloned.1.call-done, f32[4096]{0:T(1024)} %param.12, f32[512]{0:T(512)S(1)} %add_rsqrt_fusion), kind=kOutput, calls=%fused_computation.100 | convolution fusion | flops 2155872256 | bytes 9455616 | tf_op jit(solution)/shard_map/dot_general | solution.py:166
  76.7 6.5 %fusion.7 = bf16[512,512]{0,1:T(8,128)(2,1)S(1)} fusion(f32[512,512]{0,1:T(8,128)} %fusion.30, bf16[512,512]{1,0:T(8,128)(2,1)S(1)} %copy-done.7, bf16[4096,512]{1,0:T(8,128)(2,1)} %param.17, s32[512]{0:T(512)S(1)} %add_select_fusion, s32[512]{0:T(512)S(1)} %select_reduce_fusion.1, bf16[512,4096]{1,0:T(8,128)(2,1)} %all-gather.2.cloned.1.call-done, ...), kind=kOutput, calls=%fused_computation.20 | convolution fusion | flops 2425880576 | bytes 10508288 | tf_op jit(solution)/shard_map/dot_general | solution.py:176
  83.6 0.2 copy.29
  83.8 1.6 collective-permute-start.2
  85.6 0.6 collective-permute-start.1
  86.2 0.9 copy.27
  87.1 1.5 collective-permute-start
  88.9 7.0 %collective-permute-done.2 = bf16[3,512,128]{2,1,0:T(8,128)(2,1)S(1)} collective-permute-done((bf16[3,512,128]{2,1,0:T(8,128)(2,1)S(1)}, bf16[3,512,128]{2,1,0:T(8,128)(2,1)S(1)}, u32[]{:S(2)}, u32[]{:S(2)}) %collective-permute-start.2) | collective-permute-done | bytes 393248 | tf_op jit(solution)/shard_map/ppermute | solution.py:207
  95.9 9.2 %collective-permute-done.1 = bf16[3,512,128]{2,1,0:T(8,128)(2,1)S(1)} collective-permute-done((bf16[3,512,128]{2,1,0:T(8,128)(2,1)S(1)}, bf16[3,512,128]{2,1,0:T(8,128)(2,1)S(1)}, u32[]{:S(2)}, u32[]{:S(2)}) %collective-permute-start.1) | collective-permute-done | bytes 393248 | tf_op jit(solution)/shard_map/ppermute | solution.py:207
  105.1 0.7 copy-done.3
  106.0 1.3 pad_maximum_fusion.1
  107.3 1.9 gather_fusion
  109.2 1.6 select_bitcast_fusion
  110.9 1.0 copy.30
  111.9 1.3 collective-permute-start.4
  113.2 5.3 %collective-permute-start.5 = (bf16[2,2048,128]{2,1,0:T(8,128)(2,1)}, bf16[2,2048,128]{2,1,0:T(8,128)(2,1)}, u32[]{:S(2)}, u32[]{:S(2)}) collective-permute-start(bf16[2,2048,128]{2,1,0:T(8,128)(2,1)} %bitcast.22), channel_id=1, source_target_pairs={{0,48},{4,52},{8,56},{12,60},{16,64},{20,68},{24,72},{28,76},{32,8... | collective-permute-start | bytes 3145736 | tf_op jit(solution)/shard_map/ppermute | solution.py:221
  118.9 1.0 slice.59
  119.8 1.9 collective-permute-start.6
  121.8 1.4 collective-permute-start.3
  123.2 1.9 collective-permute-start.7
  125.3 0.4 copy.31.start_ref
  125.8 1.0 constant_dynamic-update-slice_fusion.5
  126.8 62.5 %collective-permute-done.4 = bf16[2,2048,128]{2,1,0:T(8,128)(2,1)} collective-permute-done((bf16[2,2048,128]{2,1,0:T(8,128)(2,1)}, bf16[2,2048,128]{2,1,0:T(8,128)(2,1)}, u32[]{:S(2)}, u32[]{:S(2)}) %collective-permute-start.4) | collective-permute-done | bytes 1048608 | tf_op jit(solution)/shard_map/ppermute | solution.py:221
  189.3 1.4 constant_dynamic-update-slice_fusion.4
  190.7 1.4 constant_dynamic-update-slice_fusion.3
  192.0 14.8 %collective-permute-done.6 = bf16[2,2048,128]{2,1,0:T(8,128)(2,1)} collective-permute-done((bf16[2,2048,128]{2,1,0:T(8,128)(2,1)}, bf16[2,2048,128]{2,1,0:T(8,128)(2,1)}, u32[]{:S(2)}, u32[]{:S(2)}) %collective-permute-start.6) | collective-permute-done | bytes 1048608 | tf_op jit(solution)/shard_map/ppermute | solution.py:221
  206.8 1.4 constant_dynamic-update-slice_fusion.2
  208.2 1.4 constant_dynamic-update-slice_fusion.1
  209.6 1.4 constant_dynamic-update-slice_fusion
  210.9 1.7 slice_bitcast_fusion
  212.7 28.1 %shard_map.109 = bf16[2048,128]{1,0:T(8,128)(2,1)S(1)} custom-call(s32[6]{0:T(128)S(1)} %pad_add_fusion.1.meta, bf16[2048,128]{1,0:T(8,128)(2,1)S(1)} %bitcast.59, bf16[10752,128]{1,0:T(8,128)(2,1)S(1)} %get-tuple-element.8.k_ref, bf16[10752,128]{1,0:T(8,128)(2,1)} %get-tuple-element.7.v_ref, s32[2048,1]{1,0:T(8,128)S(1)} %copy.31.start_ref), custom_call_target="tpu_custom_call" | custom-call | tf_op jit(solution)/shard_map/pallas_call | solution.py:128
  240.8 2.2 collective-permute-start.10
  243.1 0.5 collective-permute-start.9
  243.7 3.3 %collective-permute-done.10 = bf16[512,128]{1,0:T(8,128)(2,1)S(1)} collective-permute-done((bf16[512,128]{1,0:T(8,128)(2,1)S(1)}, bf16[512,128]{1,0:T(8,128)(2,1)S(1)}, u32[]{:S(2)}, u32[]{:S(2)}) %collective-permute-start.10) | collective-permute-done | bytes 131104 | tf_op jit(solution)/shard_map/ppermute | solution.py:230
  247.0 4.0 %collective-permute-done.9 = bf16[512,128]{1,0:T(8,128)(2,1)S(1)} collective-permute-done((bf16[512,128]{1,0:T(8,128)(2,1)S(1)}, bf16[512,128]{1,0:T(8,128)(2,1)S(1)}, u32[]{:S(2)}, u32[]{:S(2)}) %collective-permute-start.9) | collective-permute-done | bytes 131104 | tf_op jit(solution)/shard_map/ppermute | solution.py:230
  251.1 0.6 gather_fusion.1
  251.8 1.0 copy_bitcast_fusion
  (53 shorter events, 2.3 us)
Async XLA Ops:
  6.5 54.6 %copy-start = (bf16[512,512]{1,0:T(8,128)(2,1)S(1)}, bf16[512,512]{1,0:T(8,128)(2,1)}, u32[]{:S(2)}) copy-start(bf16[512,512]{1,0:T(8,128)(2,1)} %param.18) | copy-start | bytes 1572868
  6.5 45.9 %copy-start.8 = (f32[4096]{0:T(1024)S(1)}, f32[4096]{0:T(1024)}, u32[]{:S(2)}) copy-start(f32[4096]{0:T(1024)} %param.12) | copy-start | bytes 49156
  6.5 42.6 %all-gather.2.cloned.1.call-start = ((), (), s32[]{:S(2)}) async-start(), calls=%async_computation | async-start | bytes 5242880 | tf_op jit(solution)/shard_map/all_gather | solution.py:158
  49.2 3.4 %copy-start.1 = (bf16[512,4096]{1,0:T(8,128)(2,1)S(1)}, bf16[512,4096]{1,0:T(8,128)(2,1)}, u32[]{:S(2)}) copy-start(bf16[512,4096]{1,0:T(8,128)(2,1)} %all-gather.2.cloned.1.call-done) | copy-start | bytes 12582916
  52.6 5.9 %copy-start.6 = (bf16[4096,512]{1,0:T(8,128)(2,1)S(1)}, bf16[4096,512]{1,0:T(8,128)(2,1)}, u32[]{:S(2)}) copy-start(bf16[4096,512]{1,0:T(8,128)(2,1)} %param.14) | copy-start | bytes 12582916
  69.6 7.1 %copy-start.7 = (bf16[512,512]{1,0:T(8,128)(2,1)S(1)}, bf16[512,512]{1,0:T(8,128)(2,1)}, u32[]{:S(2)}) copy-start(bf16[512,512]{1,0:T(8,128)(2,1)} %param.19) | copy-start | bytes 1572868
  69.6 7.1 %copy-start.9 = (f32[4096]{0:T(1024)S(1)}, f32[4096]{0:T(1024)}, u32[]{:S(2)}) copy-start(f32[4096]{0:T(1024)} %param.12) | copy-start | bytes 49156
  76.7 6.5 %copy-start.2 = (bf16[1,512,4,64]{1,3,2,0:T(8,128)(2,1)S(1)}, bf16[1,512,4,64]{1,3,2,0:T(8,128)(2,1)}, u32[]{:S(2)}) copy-start(bf16[1,512,4,64]{1,3,2,0:T(8,128)(2,1)} %get-tuple-element.22) | copy-start | bytes 786436
  83.8 12.1 %collective-permute-start.2 = (bf16[3,512,128]{2,1,0:T(8,128)(2,1)S(1)}, bf16[3,512,128]{2,1,0:T(8,128)(2,1)S(1)}, u32[]{:S(2)}, u32[]{:S(2)}) collective-permute-start(bf16[3,512,128]{2,1,0:T(8,128)(2,1)S(1)} %bitcast.68), channel_id=1, source_target_pairs={{0,12},{4,0},{8,4},{12,8},{16,28},{20,16},{24,20},{28,24},{32,44},... | collective-permute-start | bytes 1179656 | tf_op jit(solution)/shard_map/ppermute | solution.py:207
  85.6 19.5 %collective-permute-start.1 = (bf16[3,512,128]{2,1,0:T(8,128)(2,1)S(1)}, bf16[3,512,128]{2,1,0:T(8,128)(2,1)S(1)}, u32[]{:S(2)}, u32[]{:S(2)}) collective-permute-start(bf16[3,512,128]{2,1,0:T(8,128)(2,1)S(1)} %bitcast.69), channel_id=1, source_target_pairs={{0,8},{4,12},{8,0},{12,4},{16,24},{20,28},{24,16},{28,20},{32,40},... | collective-permute-start | bytes 1179656 | tf_op jit(solution)/shard_map/ppermute | solution.py:207
  87.1 17.9 %collective-permute-start = (bf16[3,512,128]{2,1,0:T(8,128)(2,1)}, bf16[3,512,128]{2,1,0:T(8,128)(2,1)S(1)}, u32[]{:S(2)}, u32[]{:S(2)}) collective-permute-start(bf16[3,512,128]{2,1,0:T(8,128)(2,1)} %bitcast.70), channel_id=1, source_target_pairs={{0,4},{4,8},{8,12},{12,0},{16,20},{20,24},{24,28},{28,16},{32,36},... | collective-permute-start | bytes 1179656 | tf_op jit(solution)/shard_map/ppermute | solution.py:207
  105.1 0.7 copy-start.3
  105.1 0.9 copy-start.4
  109.2 9.5 %copy-start.5 = (s32[16]{0:T(128)S(1)}, s32[16]{0:T(128)}, u32[]{:S(2)}) copy-start(s32[16]{0:T(128)} %param.20) | copy-start | bytes 196
  111.9 77.3 %collective-permute-start.4 = (bf16[2,2048,128]{2,1,0:T(8,128)(2,1)}, bf16[2,2048,128]{2,1,0:T(8,128)(2,1)}, u32[]{:S(2)}, u32[]{:S(2)}) collective-permute-start(bf16[2,2048,128]{2,1,0:T(8,128)(2,1)} %bitcast.22), channel_id=1, source_target_pairs={{0,64},{4,68},{8,72},{12,76},{16,80},{20,84},{24,88},{28,92},{32,9... | collective-permute-start | bytes 3145736 | tf_op jit(solution)/shard_map/ppermute | solution.py:221
  113.2 77.4 %collective-permute-start.5 = (bf16[2,2048,128]{2,1,0:T(8,128)(2,1)}, bf16[2,2048,128]{2,1,0:T(8,128)(2,1)}, u32[]{:S(2)}, u32[]{:S(2)}) collective-permute-start(bf16[2,2048,128]{2,1,0:T(8,128)(2,1)} %bitcast.22), channel_id=1, source_target_pairs={{0,48},{4,52},{8,56},{12,60},{16,64},{20,68},{24,72},{28,76},{32,8... | collective-permute-start | bytes 3145736 | tf_op jit(solution)/shard_map/ppermute | solution.py:221
  119.8 87.0 %collective-permute-start.6 = (bf16[2,2048,128]{2,1,0:T(8,128)(2,1)}, bf16[2,2048,128]{2,1,0:T(8,128)(2,1)}, u32[]{:S(2)}, u32[]{:S(2)}) collective-permute-start(bf16[2,2048,128]{2,1,0:T(8,128)(2,1)} %bitcast.22), channel_id=1, source_target_pairs={{0,32},{4,36},{8,40},{12,44},{16,48},{20,52},{24,56},{28,60},{32,6... | collective-permute-start | bytes 3145736 | tf_op jit(solution)/shard_map/ppermute | solution.py:221
  121.8 4.0 %collective-permute-start.3 = (bf16[2,512,128]{2,1,0:T(8,128)(2,1)S(1)}, bf16[2,512,128]{2,1,0:T(8,128)(2,1)}, u32[]{:S(2)}, u32[]{:S(2)}) collective-permute-start(bf16[2,512,128]{2,1,0:T(8,128)(2,1)S(1)} %slice.59), channel_id=1, source_target_pairs={{0,80},{4,84},{8,88},{12,92},{16,96},{20,100},{24,104},{28,108},{3... | collective-permute-start | bytes 786440 | tf_op jit(solution)/shard_map/ppermute | solution.py:221
  123.2 85.0 %collective-permute-start.7 = (bf16[2,2048,128]{2,1,0:T(8,128)(2,1)}, bf16[2,2048,128]{2,1,0:T(8,128)(2,1)}, u32[]{:S(2)}, u32[]{:S(2)}) collective-permute-start(bf16[2,2048,128]{2,1,0:T(8,128)(2,1)} %bitcast.22), channel_id=1, source_target_pairs={{0,16},{4,20},{8,24},{12,28},{16,32},{20,36},{24,40},{28,44},{32,4... | collective-permute-start | bytes 3145736 | tf_op jit(solution)/shard_map/ppermute | solution.py:221
  240.8 6.2 %collective-permute-start.10 = (bf16[512,128]{1,0:T(8,128)(2,1)S(1)}, bf16[512,128]{1,0:T(8,128)(2,1)S(1)}, u32[]{:S(2)}, u32[]{:S(2)}) collective-permute-start(bf16[512,128]{1,0:T(8,128)(2,1)S(1)} %get-tuple-element.18), channel_id=1, source_target_pairs={{0,12},{4,0},{8,4},{12,8},{16,28},{20,16},{24,20},{28,24},{32,44},... | collective-permute-start | bytes 393224 | tf_op jit(solution)/shard_map/ppermute | solution.py:230
  243.1 8.0 %collective-permute-start.9 = (bf16[512,128]{1,0:T(8,128)(2,1)S(1)}, bf16[512,128]{1,0:T(8,128)(2,1)S(1)}, u32[]{:S(2)}, u32[]{:S(2)}) collective-permute-start(bf16[512,128]{1,0:T(8,128)(2,1)S(1)} %get-tuple-element.19), channel_id=1, source_target_pairs={{0,8},{4,12},{8,0},{12,4},{16,24},{20,28},{24,16},{28,20},{32,40},... | collective-permute-start | bytes 393224 | tf_op jit(solution)/shard_map/ppermute | solution.py:230
  243.6 7.4 %collective-permute-start.8 = (bf16[512,128]{1,0:T(8,128)(2,1)S(1)}, bf16[512,128]{1,0:T(8,128)(2,1)S(1)}, u32[]{:S(2)}, u32[]{:S(2)}) collective-permute-start(bf16[512,128]{1,0:T(8,128)(2,1)S(1)} %get-tuple-element.20), channel_id=1, source_target_pairs={{0,4},{4,8},{8,12},{12,0},{16,20},{20,24},{24,28},{28,16},{32,36},... | collective-permute-start | bytes 393224 | tf_op jit(solution)/shard_map/ppermute | solution.py:230
Sparse Core Ops, SparseCore 0:
  9.0 40.1 all-gather.1
where the time goes:
time: 262 us; the launch traced here: 260 us
  waiting for transfers between devices  140 us (53%)
  matrix products  28.5 us (11%)
  Pallas kernels  28.1 us (11%)
  local copies, waits for them, and re-layouts  18.5 us (7%)
  starting transfers between devices  18.4 us (7%)
  between operations  13.8 us (5%)
  other arithmetic  12.4 us (5%)
    ppermute x5, waiting for transfers between devices, body(): segments.insert(0, lax.ppermute(key_value[:, span - rows:], 'req', pairs))  77.3 us
    all_gather x1, waiting for transfers between devices, body(): whole = lax.all_gather(tokens, 'tp', axis=1, tiled=True)  38.2 us
    pallas_call x1, Pallas kernels, flash_attention(): pl.pallas_call(flash_kernel, grid_spec=grid_spec, out_shape=jax.ShapeDtyp...  28.1 us
    ppermute x6, waiting for transfers between devices, body(): parts.append(lax.ppermute(sent, 'req', group_pairs(step)))  23.5 us
    dot_general x3, matrix products, body(): jnp.dot(normed, weight, preferred_element_type=jnp.float32)  15.6 us
    ppermute x5, starting transfers between devices, body(): segments.insert(0, lax.ppermute(key_value[:, span - rows:], 'req', pairs))  11.8 us
    unnamed x25, local copies, waits for them, and re-layouts  7.51 us
    ppermute x6, starting transfers between devices, body(): parts.append(lax.ppermute(sent, 'req', group_pairs(step)))  6.55 us
  transfers between devices with their start and end apart: 12, of which 7 were waited for; matrix products, arithmetic and copies ran while one was open for 5% of the time, Pallas kernels for 0%

commit v1 on v0

--- a/solution.py
+++ b/solution.py
@@ -54,7 +54,9 @@
 KEY_TILE = 512
 
 
-def flash_kernel(meta, q_ref, k_ref, v_ref, start_ref, o_ref, peak_ref, total_ref, acc_ref):
+def flash_kernel(
+    meta, q_ref, k_ref, v_ref, start_ref, peak_in, total_in, acc_in, peak_ref, total_ref, acc_ref
+):
     i = pl.program_id(0)
     j = pl.program_id(1)
     lo = meta[2 + 2 * i]
@@ -62,9 +64,9 @@
 
     @pl.when(j == 0)
     def _():
-        peak_ref[...] = jnp.full(peak_ref.shape, MASKED, jnp.float32)
-        total_ref[...] = jnp.zeros(total_ref.shape, jnp.float32)
-        acc_ref[...] = jnp.zeros(acc_ref.shape, jnp.float32)
+        peak_ref[...] = peak_in[...]
+        total_ref[...] = total_in[...]
+        acc_ref[...] = acc_in[...]
 
     @pl.when(lo + j <= hi)
     def _():
@@ -86,53 +88,50 @@
         )
         peak_ref[...] = new_peak
 
-    @pl.when(j == pl.num_programs(1) - 1)
-    def _():
-        o_ref[...] = (acc_ref[...] / total_ref[...]).astype(o_ref.dtype)
-
-
-def flash_attention(queries, keys, values, query_first, key_base, lengths):
+
+def flash_step(state, queries, starts, key_value, query_first, key_base):
     query_rows = queries.shape[0]
-    key_rows = keys.shape[0]
+    key_rows = key_value.shape[1]
     q_tiles = query_rows // QUERY_TILE
     k_tiles = key_rows // KEY_TILE
     positions = query_first + jnp.arange(query_rows, dtype=jnp.int32)
-    starts, _ = prompt_layout(lengths, positions)
-    tile_first = starts[::QUERY_TILE]
+    tile_first = starts[::QUERY_TILE, 0]
     tile_last = positions[QUERY_TILE - 1 :: QUERY_TILE]
-    lo = jnp.clip((tile_first - key_base) // KEY_TILE, 0, k_tiles - 1)
-    hi = jnp.clip((tile_last - key_base) // KEY_TILE, 0, k_tiles - 1)
+    lo = jnp.maximum((tile_first - key_base) // KEY_TILE, 0)
+    hi = jnp.minimum((tile_last - key_base) // KEY_TILE, k_tiles - 1)
     meta = jnp.concatenate(
         [jnp.stack([query_first, key_base]).astype(jnp.int32), jnp.stack([lo, hi], 1).reshape(-1)]
     ).astype(jnp.int32)
 
     def key_map(i, j, meta):
-        return (jnp.minimum(meta[2 + 2 * i] + j, meta[3 + 2 * i]), 0)
-
+        block = jnp.minimum(meta[2 + 2 * i] + j, meta[3 + 2 * i])
+        return (0, jnp.clip(block, 0, k_tiles - 1), 0)
+
+    row_spec = pl.BlockSpec((QUERY_TILE, 1), lambda i, j, meta: (i, 0))
+    acc_spec = pl.BlockSpec((QUERY_TILE, HEAD), lambda i, j, meta: (i, 0))
     grid_spec = pltpu.PrefetchScalarGridSpec(
         num_scalar_prefetch=1,
         grid=(q_tiles, k_tiles),
         in_specs=[
             pl.BlockSpec((QUERY_TILE, HEAD), lambda i, j, meta: (i, 0)),
-            pl.BlockSpec((KEY_TILE, HEAD), key_map),
-            pl.BlockSpec((KEY_TILE, HEAD), key_map),
-            pl.BlockSpec((QUERY_TILE, 1), lambda i, j, meta: (i, 0)),
+            pl.BlockSpec((None, KEY_TILE, HEAD), key_map),
+            pl.BlockSpec((None, KEY_TILE, HEAD), lambda i, j, meta: (1,) + key_map(i, j, meta)[1:]),
+            row_spec,
+            row_spec,
+            row_spec,
+            acc_spec,
         ],
-        out_specs=pl.BlockSpec((QUERY_TILE, HEAD), lambda i, j, meta: (i, 0)),
-        scratch_shapes=[
-            pltpu.VMEM((QUERY_TILE, 1), jnp.float32),
-            pltpu.VMEM((QUERY_TILE, 1), jnp.float32),
-            pltpu.VMEM((QUERY_TILE, HEAD), jnp.float32),
-        ],
+        out_specs=[row_spec, row_spec, acc_spec],
     )
     return pl.pallas_call(
         flash_kernel,
         grid_spec=grid_spec,
-        out_shape=jax.ShapeDtypeStruct((query_rows, HEAD), jnp.bfloat16),
+        out_shape=[jax.ShapeDtypeStruct(s.shape, jnp.float32) for s in state],
+        input_output_aliases={5: 0, 6: 1, 7: 2},
         compiler_params=pltpu.CompilerParams(
             dimension_semantics=("arbitrary", "arbitrary"), vmem_limit_bytes=48 * 1024 * 1024
         ),
-    )(meta, queries, keys, values, starts.reshape(query_rows, 1))
+    )(meta, queries, key_value, key_value, starts, *state)
 
 
 def body(
@@ -212,16 +211,26 @@
 
     chunk_count = req_count // group
     reach = MAXLEN - 1
-    segments = [key_value]
+    span_positions = chunk * span + jnp.arange(span, dtype=jnp.int32)
+    span_starts, _ = prompt_layout(lengths, span_positions)
+    span_starts = span_starts.reshape(span, 1)
+    state = (
+        jnp.full((span, 1), MASKED, jnp.float32),
+        jnp.zeros((span, 1), jnp.float32),
+        jnp.zeros((span, HEAD), jnp.float32),
+    )
+    arrived = [(key_value, chunk * span)]
     for back in range(1, chunk_count):
         if (back - 1) * span >= reach:
             break
         rows = min(span, -(-(reach - (back - 1) * span) // KEY_TILE) * KEY_TILE)
         pairs = [(i, i + back * group) for i in range(req_count - back * group)]
-        segments.insert(0, lax.ppermute(key_value[:, span - rows :], "req", pairs))
-    window = jnp.concatenate(segments, axis=1)
-    key_base = chunk * span + span - window.shape[1]
-    attended = flash_attention(query_span, window[0], window[1], chunk * span, key_base, lengths)
+        segment = lax.ppermute(key_value[:, span - rows :], "req", pairs)
+        arrived.append((segment, (chunk - back) * span + span - rows))
+    for segment, key_base in arrived:
+        state = flash_step(state, query_span, span_starts, segment, chunk * span, key_base)
+    peak, total, summed = state
+    attended = (summed / total).astype(jnp.bfloat16)
     attended = attended.reshape(group, row_count, HEAD)
 
     parts = [lax.dynamic_index_in_dim(attended, member, axis=0, keepdims=False)]

time: 262 us -> 231 us (0.88)
  the two profiles are of different devices: /device:TPU:64 before, /device:TPU:68 now
where the time goes in v1:
time: 231 us
  waiting for transfers between devices  94.5 us (41%)
  Pallas kernels  41.7 us (18%)
  matrix products  28.6 us (12%)
  starting transfers between devices  23.8 us (10%)
  other arithmetic  14.8 us (6%)
  between operations  13.9 us (6%)
  local copies, waits for them, and re-layouts  13.7 us (6%)
    pallas_call x6, Pallas kernels, flash_step(): pl.pallas_call(flash_kernel, grid_spec=grid_spec, out_shape=[jax.ShapeDty...  41.7 us
    ppermute x5, waiting for transfers between devices, body(): segment = lax.ppermute(key_value[:, span - rows:], 'req', pairs)  41.6 us
    all_gather x1, waiting for transfers between devices, body(): whole = lax.all_gather(tokens, 'tp', axis=1, tiled=True)  33.2 us
    ppermute x6, waiting for transfers between devices, body(): parts.append(lax.ppermute(sent, 'req', group_pairs(step)))  19 us
    dot_general x3, matrix products, body(): jnp.dot(normed, weight, preferred_element_type=jnp.float32)  15.7 us
    ppermute x6, starting transfers between devices, body(): parts.append(lax.ppermute(sent, 'req', group_pairs(step)))  12.2 us
    ppermute x5, starting transfers between devices, body(): segment = lax.ppermute(key_value[:, span - rows:], 'req', pairs)  11.7 us
    dot_general x1, matrix products, body(): jnp.dot(value_middle, value_up_maps, preferred_element_type=jnp.float32)  6.49 us
  transfers between devices with their start and end apart: 12, of which 8 were waited for; matrix products, arithmetic and copies ran while one was open for 5% of the time, Pallas kernels for 18%

profile of v1, /device:TPU:68, one launch (start us, length us, event | category | flops | bytes accessed | tf_op | source)
XLA Modules:
  0.0 230.9 jit_solution(16095987685848992849)
XLA Ops:
  6.5 0.7 all-gather.2.cloned.1.call-update
  7.3 0.7 copy.76
  8.2 0.6 slice.42
  8.9 0.8 select_reduce_fusion
  10.8 0.7 fusion.19
  11.6 0.7 select_reduce_fusion.1
  12.3 1.2 multiply_cosine_fusion
  13.5 33.2 %all-gather.2.cloned.1.call-done = bf16[512,4096]{1,0:T(8,128)(2,1)} async-done(((bf16[512,1024]{1,0:T(8,128)(2,1)}), bf16[512,4096]{1,0:T(8,128)(2,1)}) %all-gather.2.cloned.1.call-update) | async-done | bytes 4194320 | tf_op jit(solution)/shard_map/all_gather | solution.py:157
  46.7 3.2 %fusion = f32[512]{0:T(512)S(1)} fusion(bf16[512,4096]{1,0:T(8,128)(2,1)} %all-gather.2.cloned.1.call-done), kind=kLoop, calls=%fused_computation.4 | loop fusion | flops 6290944 | bytes 4196352 | tf_op jit(solution)/shard_map/reduce_sum | solution.py:161
  50.1 5.9 %fusion.42 = f32[512,512]{0,1:T(8,128)} fusion(bf16[4096,512]{1,0:T(8,128)(2,1)} %param.13, bf16[512,4096]{1,0:T(8,128)(2,1)S(1)} %copy-done.2, f32[4096]{0:T(1024)S(1)} %copy-done.13, f32[512]{0:T(512)S(1)} %add_rsqrt_fusion), kind=kOutput, calls=%fused_computation.155 | convolution fusion | flops 2155872256 | bytes 9455616 | tf_op jit(solution)/shard_map/dot_general | solution.py:165
  56.1 2.6 %fusion.38 = f32[512,512]{0,1:T(8,128)S(1)} fusion(bf16[4096,512]{1,0:T(8,128)(2,1)S(1)} %copy-done.11, bf16[512,4096]{1,0:T(8,128)(2,1)S(1)} %copy-done.2, f32[4096]{0:T(1024)S(1)} %copy-done.13, f32[512]{0:T(512)S(1)} %add_rsqrt_fusion), kind=kOutput, calls=%fused_computation.154 | convolution fusion | flops 2155872256 | bytes 9455616 | tf_op jit(solution)/shard_map/dot_general | solution.py:165
  58.7 6.4 %fusion.4 = f32[512,512]{0,1:T(8,128)S(1)} fusion(f32[512,512]{0,1:T(8,128)} %fusion.42, bf16[512,512]{1,0:T(8,128)(2,1)S(1)} %copy-done, bf16[4096,512]{1,0:T(8,128)(2,1)} %param.16, s32[512]{0:T(512)S(1)} %add_select_fusion, s32[512]{0:T(512)S(1)} %select_reduce_fusion.1, bf16[512,4096]{1,0:T(8,128)(2,1)} %all-gather.2.cloned.1.call-done, ...), kind=kOutput, calls=%fused_computation.13 | convolution fusion | flops 2425618432 | bytes 11032576 | tf_op jit(solution)/shard_map/dot_general | solution.py:170
  65.1 2.0 fusion.14
  67.1 7.2 %fusion.36 = f32[512,512]{0,1:T(8,128)} fusion(bf16[4096,512]{1,0:T(8,128)(2,1)} %param.15, bf16[512,4096]{1,0:T(8,128)(2,1)} %all-gather.2.cloned.1.call-done, f32[4096]{0:T(1024)} %param.12, f32[512]{0:T(512)} %copy-done.6), kind=kOutput, calls=%fused_computation.153 | convolution fusion | flops 2155872256 | bytes 9455616 | tf_op jit(solution)/shard_map/dot_general | solution.py:165
  74.3 6.5 %fusion.7 = bf16[512,512]{0,1:T(8,128)(2,1)S(1)} fusion(f32[512,512]{0,1:T(8,128)} %fusion.36, bf16[512,512]{1,0:T(8,128)(2,1)S(1)} %copy-done.12, bf16[4096,512]{1,0:T(8,128)(2,1)} %param.17, s32[512]{0:T(512)S(1)} %add_select_fusion, s32[512]{0:T(512)S(1)} %select_reduce_fusion.1, bf16[512,4096]{1,0:T(8,128)(2,1)} %all-gather.2.cloned.1.call-done, ...), kind=kOutput, calls=%fused_computation.18 | convolution fusion | flops 2425880576 | bytes 10508288 | tf_op jit(solution)/shard_map/dot_general | solution.py:175
  81.4 2.1 collective-permute-start
  83.8 1.6 collective-permute-start.1
  85.4 0.9 copy.81
  86.3 0.9 collective-permute-start.2
  87.4 7.1 %collective-permute-done = bf16[3,512,128]{2,1,0:T(8,128)(2,1)S(1)} collective-permute-done((bf16[3,512,128]{2,1,0:T(8,128)(2,1)S(1)}, bf16[3,512,128]{2,1,0:T(8,128)(2,1)S(1)}, u32[]{:S(2)}, u32[]{:S(2)}) %collective-permute-start) | collective-permute-done | bytes 393248 | tf_op jit(solution)/shard_map/ppermute | solution.py:206
  94.5 7.9 %collective-permute-done.1 = bf16[3,512,128]{2,1,0:T(8,128)(2,1)S(1)} collective-permute-done((bf16[3,512,128]{2,1,0:T(8,128)(2,1)S(1)}, bf16[3,512,128]{2,1,0:T(8,128)(2,1)S(1)}, u32[]{:S(2)}, u32[]{:S(2)}) %collective-permute-start.1) | collective-permute-done | bytes 393248 | tf_op jit(solution)/shard_map/ppermute | solution.py:206
  102.4 0.7 copy-done.4
  103.3 1.3 pad_maximum_fusion.1
  104.6 1.9 gather_fusion
  106.5 1.6 select_bitcast_fusion
  108.2 1.1 copy.82
  109.3 4.6 %collective-permute-start.7 = (bf16[2,2048,128]{2,1,0:T(8,128)(2,1)}, bf16[2,2048,128]{2,1,0:T(8,128)(2,1)}, u32[]{:S(2)}, u32[]{:S(2)}) collective-permute-start(bf16[2,2048,128]{2,1,0:T(8,128)(2,1)} %bitcast.22.k_ref.v_ref), channel_id=1, source_target_pairs={{0,16},{4,20},{8,24},{12,28},{16,32},{20,36},{24,40},{28,44},{32,4... | collective-permute-start | bytes 3145736 | tf_op jit(solution)/shard_map/ppermute | solution.py:228
  113.9 3.2 %collective-permute-start.6 = (bf16[2,2048,128]{2,1,0:T(8,128)(2,1)}, bf16[2,2048,128]{2,1,0:T(8,128)(2,1)}, u32[]{:S(2)}, u32[]{:S(2)}) collective-permute-start(bf16[2,2048,128]{2,1,0:T(8,128)(2,1)} %bitcast.22.k_ref.v_ref), channel_id=1, source_target_pairs={{0,32},{4,36},{8,40},{12,44},{16,48},{20,52},{24,56},{28,60},{32,6... | collective-permute-start | bytes 3145736 | tf_op jit(solution)/shard_map/ppermute | solution.py:228
  117.1 1.9 collective-permute-start.5
  119.0 1.3 collective-permute-start.4
  121.4 1.7 slice.61
  123.0 0.7 collective-permute-start.3
  123.8 1.4 copy.95.start_ref
  125.9 0.8 copy-done.1
  126.7 15.0 %shard_map.109 = (f32[2048,1]{1,0:T(8,128)S(1)}, f32[2048,1]{1,0:T(8,128)S(1)}, f32[2048,128]{1,0:T(8,128)S(1)}) custom-call(s32[6]{0:T(128)S(1)} %pad_add_fusion.11.meta, bf16[2048,128]{1,0:T(8,128)(2,1)S(1)} %bitcast.67, bf16[2,2048,128]{2,1,0:T(8,128)(2,1)} %bitcast.22.k_ref.v_ref, ...), custom_call_target="tpu_custom_call", output_to_operand_aliasing={{0}: (5, {}), {1}: (6, {}), {2}: (7, {})} | custom-call | tf_op jit(solution)/shard_map/pallas_call | solution.py:126
  141.8 18.1 %shard_map.110 = (f32[2048,1]{1,0:T(8,128)S(1)}, f32[2048,1]{1,0:T(8,128)S(1)}, f32[2048,128]{1,0:T(8,128)S(1)}) custom-call(s32[6]{0:T(128)S(1)} %pad_add_fusion.10.meta, bf16[2048,128]{1,0:T(8,128)(2,1)S(1)} %bitcast.68, bf16[2,2048,128]{2,1,0:T(8,128)(2,1)} %collective-permute-done.7.k_ref.v_ref, ...), custom_call_target="tpu_custom_call", output_to_operand_aliasing={{0}: (5, {}), {1}: (6, {}), {2}: (7, {})} | custom-call | tf_op jit(solution)/shard_map/pallas_call | solution.py:126
  159.9 24.2 %collective-permute-done.6.k_ref.v_ref = bf16[2,2048,128]{2,1,0:T(8,128)(2,1)} collective-permute-done((bf16[2,2048,128]{2,1,0:T(8,128)(2,1)}, bf16[2,2048,128]{2,1,0:T(8,128)(2,1)}, u32[]{:S(2)}, u32[]{:S(2)}) %collective-permute-start.6) | collective-permute-done | bytes 1048608 | tf_op jit(solution)/shard_map/ppermute | solution.py:228
  184.0 2.5 %shard_map.111 = (f32[2048,1]{1,0:T(8,128)S(1)}, f32[2048,1]{1,0:T(8,128)S(1)}, f32[2048,128]{1,0:T(8,128)S(1)}) custom-call(s32[6]{0:T(128)S(1)} %pad_add_fusion.9.meta, bf16[2048,128]{1,0:T(8,128)(2,1)S(1)} %bitcast.69, bf16[2,2048,128]{2,1,0:T(8,128)(2,1)} %collective-permute-done.6.k_ref.v_ref, ...), custom_call_target="tpu_custom_call", output_to_operand_aliasing={{0}: (5, {}), {1}: (6, {}), {2}: (7, {})} | custom-call | tf_op jit(solution)/shard_map/pallas_call | solution.py:126
  186.5 2.5 %shard_map.112 = (f32[2048,1]{1,0:T(8,128)S(1)}, f32[2048,1]{1,0:T(8,128)S(1)}, f32[2048,128]{1,0:T(8,128)S(1)}) custom-call(s32[6]{0:T(128)S(1)} %pad_add_fusion.8.meta, bf16[2048,128]{1,0:T(8,128)(2,1)S(1)} %bitcast.70, bf16[2,2048,128]{2,1,0:T(8,128)(2,1)} %collective-permute-done.5.k_ref.v_ref, ...), custom_call_target="tpu_custom_call", output_to_operand_aliasing={{0}: (5, {}), {1}: (6, {}), {2}: (7, {})} | custom-call | tf_op jit(solution)/shard_map/pallas_call | solution.py:126
  189.0 17.4 %collective-permute-done.4.k_ref.v_ref = bf16[2,2048,128]{2,1,0:T(8,128)(2,1)} collective-permute-done((bf16[2,2048,128]{2,1,0:T(8,128)(2,1)}, bf16[2,2048,128]{2,1,0:T(8,128)(2,1)}, u32[]{:S(2)}, u32[]{:S(2)}) %collective-permute-start.4) | collective-permute-done | bytes 1048608 | tf_op jit(solution)/shard_map/ppermute | solution.py:228
  206.4 2.5 %shard_map.113 = (f32[2048,1]{1,0:T(8,128)S(1)}, f32[2048,1]{1,0:T(8,128)S(1)}, f32[2048,128]{1,0:T(8,128)S(1)}) custom-call(s32[6]{0:T(128)S(1)} %pad_add_fusion.7.meta, bf16[2048,128]{1,0:T(8,128)(2,1)S(1)} %bitcast.71, bf16[2,2048,128]{2,1,0:T(8,128)(2,1)} %collective-permute-done.4.k_ref.v_ref, ...), custom_call_target="tpu_custom_call", output_to_operand_aliasing={{0}: (5, {}), {1}: (6, {}), {2}: (7, {})} | custom-call | tf_op jit(solution)/shard_map/pallas_call | solution.py:126
  208.9 1.1 shard_map.114
  210.8 6.0 %collective-permute-start.8 = (bf16[512,128]{1,0:T(8,128)(2,1)S(1)}, bf16[512,128]{1,0:T(8,128)(2,1)S(1)}, u32[]{:S(2)}, u32[]{:S(2)}) collective-permute-start(bf16[512,128]{1,0:T(8,128)(2,1)S(1)} %get-tuple-element.52), channel_id=1, source_target_pairs={{0,4},{4,8},{8,12},{12,0},{16,20},{20,24},{24,28},{28,16},{32,36},... | collective-permute-start | bytes 393224 | tf_op jit(solution)/shard_map/ppermute | solution.py:239
  217.4 1.0 collective-permute-start.10
  218.4 1.4 collective-permute-done.8
  219.8 2.0 collective-permute-done.9
  222.4 0.6 gather_fusion.1
  223.1 1.0 copy_bitcast_fusion
  (84 shorter events, 6.7 us)
Async XLA Ops:
  6.5 52.1 %copy-start = (bf16[512,512]{1,0:T(8,128)(2,1)S(1)}, bf16[512,512]{1,0:T(8,128)(2,1)}, u32[]{:S(2)}) copy-start(bf16[512,512]{1,0:T(8,128)(2,1)} %param.18) | copy-start | bytes 1572868
  6.5 43.4 %copy-start.13 = (f32[4096]{0:T(1024)S(1)}, f32[4096]{0:T(1024)}, u32[]{:S(2)}) copy-start(f32[4096]{0:T(1024)} %param.12) | copy-start | bytes 49156
  6.5 40.2 %all-gather.2.cloned.1.call-start = ((), (), s32[]{:S(2)}) async-start(), calls=%async_computation | async-start | bytes 5242880 | tf_op jit(solution)/shard_map/all_gather | solution.py:157
  46.7 3.4 %copy-start.2 = (bf16[512,4096]{1,0:T(8,128)(2,1)S(1)}, bf16[512,4096]{1,0:T(8,128)(2,1)}, u32[]{:S(2)}) copy-start(bf16[512,4096]{1,0:T(8,128)(2,1)} %all-gather.2.cloned.1.call-done) | copy-start | bytes 12582916
  50.1 8.5 %copy-start.6 = (f32[512]{0:T(512)}, f32[512]{0:T(512)S(1)}, u32[]{:S(2)}) copy-start(f32[512]{0:T(512)S(1)} %add_rsqrt_fusion) | copy-start | bytes 6148
  50.1 5.9 %copy-start.11 = (bf16[4096,512]{1,0:T(8,128)(2,1)S(1)}, bf16[4096,512]{1,0:T(8,128)(2,1)}, u32[]{:S(2)}) copy-start(bf16[4096,512]{1,0:T(8,128)(2,1)} %param.14) | copy-start | bytes 12582916
  67.1 7.2 %copy-start.7 = (f32[512]{0:T(512)S(1)}, f32[512]{0:T(512)}, u32[]{:S(2)}) copy-start(f32[512]{0:T(512)} %copy-done.6) | copy-start | bytes 6148
  67.1 7.2 %copy-start.12 = (bf16[512,512]{1,0:T(8,128)(2,1)S(1)}, bf16[512,512]{1,0:T(8,128)(2,1)}, u32[]{:S(2)}) copy-start(bf16[512,512]{1,0:T(8,128)(2,1)} %param.19) | copy-start | bytes 1572868
  67.1 7.2 %copy-start.14 = (f32[4096]{0:T(1024)S(1)}, f32[4096]{0:T(1024)}, u32[]{:S(2)}) copy-start(f32[4096]{0:T(1024)} %param.12) | copy-start | bytes 49156
  74.3 6.5 %copy-start.3 = (bf16[1,512,4,64]{1,3,2,0:T(8,128)(2,1)S(1)}, bf16[1,512,4,64]{1,3,2,0:T(8,128)(2,1)}, u32[]{:S(2)}) copy-start(bf16[1,512,4,64]{1,3,2,0:T(8,128)(2,1)} %get-tuple-element.54) | copy-start | bytes 786436
  80.8 6.4 %copy-start.8 = (s32[4]{0:T(128)S(1)}, s32[4]{0:T(128)}, u32[]{:S(2)}) copy-start(s32[4]{0:T(128)} %fusion.25) | copy-start | bytes 52
  80.8 6.4 %copy-start.10 = (s32[2,1]{0,1:T(1,128)S(1)}, s32[2,1]{0,1:T(1,128)}, u32[]{:S(2)}) copy-start(s32[2,1]{0,1:T(1,128)} %slice.41) | copy-start | bytes 28
  81.4 13.1 %collective-permute-start = (bf16[3,512,128]{2,1,0:T(8,128)(2,1)S(1)}, bf16[3,512,128]{2,1,0:T(8,128)(2,1)S(1)}, u32[]{:S(2)}, u32[]{:S(2)}) collective-permute-start(bf16[3,512,128]{2,1,0:T(8,128)(2,1)S(1)} %bitcast.81), channel_id=1, source_target_pairs={{0,4},{4,8},{8,12},{12,0},{16,20},{20,24},{24,28},{28,16},{32,36},... | collective-permute-start | bytes 1179656 | tf_op jit(solution)/shard_map/ppermute | solution.py:206
  83.8 18.6 %collective-permute-start.1 = (bf16[3,512,128]{2,1,0:T(8,128)(2,1)S(1)}, bf16[3,512,128]{2,1,0:T(8,128)(2,1)S(1)}, u32[]{:S(2)}, u32[]{:S(2)}) collective-permute-start(bf16[3,512,128]{2,1,0:T(8,128)(2,1)S(1)} %bitcast.82), channel_id=1, source_target_pairs={{0,8},{4,12},{8,0},{12,4},{16,24},{20,28},{24,16},{28,20},{32,40},... | collective-permute-start | bytes 1179656 | tf_op jit(solution)/shard_map/ppermute | solution.py:206
  86.3 16.2 %collective-permute-start.2 = (bf16[3,512,128]{2,1,0:T(8,128)(2,1)}, bf16[3,512,128]{2,1,0:T(8,128)(2,1)S(1)}, u32[]{:S(2)}, u32[]{:S(2)}) collective-permute-start(bf16[3,512,128]{2,1,0:T(8,128)(2,1)} %bitcast.83), channel_id=1, source_target_pairs={{0,12},{4,0},{8,4},{12,8},{16,28},{20,16},{24,20},{28,24},{32,44},... | collective-permute-start | bytes 1179656 | tf_op jit(solution)/shard_map/ppermute | solution.py:206
  102.4 0.8 copy-start.4
  102.4 0.9 copy-start.5
  106.5 13.8 %copy-start.9 = (s32[2]{0:T(128)S(1)}, s32[2]{0:T(128)}, u32[]{:S(2)}) copy-start(s32[2]{0:T(128)} %slice.42) | copy-start | bytes 28
  109.3 32.5 %collective-permute-start.7 = (bf16[2,2048,128]{2,1,0:T(8,128)(2,1)}, bf16[2,2048,128]{2,1,0:T(8,128)(2,1)}, u32[]{:S(2)}, u32[]{:S(2)}) collective-permute-start(bf16[2,2048,128]{2,1,0:T(8,128)(2,1)} %bitcast.22.k_ref.v_ref), channel_id=1, source_target_pairs={{0,16},{4,20},{8,24},{12,28},{16,32},{20,36},{24,40},{28,44},{32,4... | collective-permute-start | bytes 3145736 | tf_op jit(solution)/shard_map/ppermute | solution.py:228
  113.9 70.1 %collective-permute-start.6 = (bf16[2,2048,128]{2,1,0:T(8,128)(2,1)}, bf16[2,2048,128]{2,1,0:T(8,128)(2,1)}, u32[]{:S(2)}, u32[]{:S(2)}) collective-permute-start(bf16[2,2048,128]{2,1,0:T(8,128)(2,1)} %bitcast.22.k_ref.v_ref), channel_id=1, source_target_pairs={{0,32},{4,36},{8,40},{12,44},{16,48},{20,52},{24,56},{28,60},{32,6... | collective-permute-start | bytes 3145736 | tf_op jit(solution)/shard_map/ppermute | solution.py:228
  117.1 69.4 %collective-permute-start.5 = (bf16[2,2048,128]{2,1,0:T(8,128)(2,1)}, bf16[2,2048,128]{2,1,0:T(8,128)(2,1)}, u32[]{:S(2)}, u32[]{:S(2)}) collective-permute-start(bf16[2,2048,128]{2,1,0:T(8,128)(2,1)} %bitcast.22.k_ref.v_ref), channel_id=1, source_target_pairs={{0,48},{4,52},{8,56},{12,60},{16,64},{20,68},{24,72},{28,76},{32,8... | collective-permute-start | bytes 3145736 | tf_op jit(solution)/shard_map/ppermute | solution.py:228
  119.0 87.4 %collective-permute-start.4 = (bf16[2,2048,128]{2,1,0:T(8,128)(2,1)}, bf16[2,2048,128]{2,1,0:T(8,128)(2,1)}, u32[]{:S(2)}, u32[]{:S(2)}) collective-permute-start(bf16[2,2048,128]{2,1,0:T(8,128)(2,1)} %bitcast.22.k_ref.v_ref), channel_id=1, source_target_pairs={{0,64},{4,68},{8,72},{12,76},{16,80},{20,84},{24,88},{28,92},{32,9... | collective-permute-start | bytes 3145736 | tf_op jit(solution)/shard_map/ppermute | solution.py:228
  123.0 85.8 %collective-permute-start.3 = (bf16[2,512,128]{2,1,0:T(8,128)(2,1)}, bf16[2,512,128]{2,1,0:T(8,128)(2,1)S(1)}, u32[]{:S(2)}, u32[]{:S(2)}) collective-permute-start(bf16[2,512,128]{2,1,0:T(8,128)(2,1)} %slice.61), channel_id=1, source_target_pairs={{0,80},{4,84},{8,88},{12,92},{16,96},{20,100},{24,104},{28,108},{3... | collective-permute-start | bytes 786440 | tf_op jit(solution)/shard_map/ppermute | solution.py:228
  125.5 1.2 copy-start.1
  210.8 9.0 %collective-permute-start.8 = (bf16[512,128]{1,0:T(8,128)(2,1)S(1)}, bf16[512,128]{1,0:T(8,128)(2,1)S(1)}, u32[]{:S(2)}, u32[]{:S(2)}) collective-permute-start(bf16[512,128]{1,0:T(8,128)(2,1)S(1)} %get-tuple-element.52), channel_id=1, source_target_pairs={{0,4},{4,8},{8,12},{12,0},{16,20},{20,24},{24,28},{28,16},{32,36},... | collective-permute-start | bytes 393224 | tf_op jit(solution)/shard_map/ppermute | solution.py:239
  216.8 5.0 %collective-permute-start.9 = (bf16[512,128]{1,0:T(8,128)(2,1)S(1)}, bf16[512,128]{1,0:T(8,128)(2,1)S(1)}, u32[]{:S(2)}, u32[]{:S(2)}) collective-permute-start(bf16[512,128]{1,0:T(8,128)(2,1)S(1)} %get-tuple-element.51), channel_id=1, source_target_pairs={{0,8},{4,12},{8,0},{12,4},{16,24},{20,28},{24,16},{28,20},{32,40},... | collective-permute-start | bytes 393224 | tf_op jit(solution)/shard_map/ppermute | solution.py:239
  217.4 5.0 %collective-permute-start.10 = (bf16[512,128]{1,0:T(8,128)(2,1)S(1)}, bf16[512,128]{1,0:T(8,128)(2,1)S(1)}, u32[]{:S(2)}, u32[]{:S(2)}) collective-permute-start(bf16[512,128]{1,0:T(8,128)(2,1)S(1)} %get-tuple-element.50), channel_id=1, source_target_pairs={{0,12},{4,0},{8,4},{12,8},{16,28},{20,16},{24,20},{28,24},{32,44},... | collective-permute-start | bytes 393224 | tf_op jit(solution)/shard_map/ppermute | solution.py:239
Sparse Core Ops, SparseCore 0:
  9.0 37.6 all-gather.1
